TPU v7x, 256 devices: a whole 4x4x8 slice. The times are simulated.
256 devices in a mesh: row: 8 (over z), col: 32 (over y, x, core).
Axes of the slice: x: 4, y: 4, z: 8, core: 2. Of those that a mesh axis runs over, the one named last changes fastest.
Arguments:
- hidden_in: bfloat16 [1024, 2304], P('row', 'col'), may hold values from -40 to 40
- attn_gain: float32 [2304], P('col'), may hold values from 0.1 to 1.9
- qkv_weight: bfloat16 [2304, 6912], P('col'), may hold values from -0.125 to 0.125
- out_weight: bfloat16 [2304, 2304], P(None, 'col'), may hold values from -0.125 to 0.125
- moe_gain: float32 [2304], P('col'), may hold values from 0.1 to 1.9
- router_weight: float32 [2304, 8], P('col'), may hold values from -0.125 to 0.125
- expert_gate: bfloat16 [8, 2304, 5760], P('row', None, 'col'), may hold values from -0.125 to 0.125
- expert_up: bfloat16 [8, 2304, 5760], P('row', None, 'col'), may hold values from -0.125 to 0.125
- expert_down: bfloat16 [8, 5760, 2304], P('row', 'col'), may hold values from -0.078125 to 0.078125
- cache_keys: bfloat16 [2048, 64, 2304], P(('row', 'col')), may hold values from -400 to 400
- cache_values: bfloat16 [2048, 64, 2304], P(('row', 'col')), may hold values from -12 to 12
- block_table: int32 [8, 4, 64], P('row'), may hold values from 0 to 2047, as said below
- prefix_lengths: int32 [8, 4], P('row'), may hold values from 1024 to 4096, as said below
- prompt_lengths: int32 [8, 4], P('row'), may hold values from 1 to 64, 128 in all within a row
- routed_experts: int32 [1024, 2], P('row'), may hold values from 0 to 7, all different within a row; in each aligned block of 128 rows (0 to 127, 128 to 255, ...) at most 64 rows name the same one
Outputs:
- attn_out: bfloat16 [1024, 2304], P('row', 'col')
- moe_out: bfloat16 [1024, 2304], P('row', 'col')
- layer_out: bfloat16 [1024, 2304], P('row', 'col')
Inputs may be any that keep to these rules, and one draw needn't show every extreme that they name: `block_table`: entry [g, q, j] lies among the 8 pages that begin at (g * 32 + j % 32) * 8; the entries that fall among the same 8 pages are distinct. `prefix_lengths`: some request has exactly 4096 cached tokens. `prompt_lengths`: the 4 lengths of a group sum to 128; the longest of each group is exactly 64. `routed_experts`: the 2 experts of a token differ; among the tokens of one group no expert is named more than 64 times, and in some group an expert reaches 64; every expert is named by some token.
All inputs are finite; a program needn't handle non-finite values.
Results may differ from a plain program's by a relative error of at most 0.02.
The roundings to bfloat16 on the way count: a program that leaves them out, or rounds other values in their place, can miss the bound.
Values may be sent and summed in bfloat16 or wider, within the bound.
No kernel may reach another device: no remote copies, remote signals or barrier semaphores. Data moves between devices by JAX's collectives and lax.ppermute only.
A program may use at most 192 MiB of HBM per device.

v0:
```python
import math
import jax
import jax.numpy as jnp
from jax import lax
from jax.sharding import PartitionSpec as P

D = 2304
HEAD_DIM = 64
TOP = 2
norm_epsilon = 1e-05
residual_scale = 1.4 / math.sqrt(40.0)
rotary_base = 10000.0
masked_score = -1e30


def merged(value, axis, join):
    pieces = jax.tree.map(lambda part: lax.all_gather(part, axis), value)
    head = jax.tree.map(lambda part: part[0], pieces)
    tail = jax.tree.map(lambda part: part[1:], pieces)
    running, _ = lax.scan(lambda running, slab: (join(running, slab), None), head, tail)
    return running


def rotate(values, positions, head_dim):
    row_count = values.shape[0]
    head_count = values.shape[1] // head_dim
    half_dim = head_dim // 2
    frequency = rotary_base ** (-2.0 * jnp.arange(half_dim, dtype=jnp.float32) / head_dim)
    angles = positions.astype(jnp.float32)[:, None] * frequency[None, :]
    cosine = jnp.cos(angles)[:, None, :]
    sine_part = jnp.sin(angles)[:, None, :]
    shaped = values.reshape(row_count, head_count, head_dim)
    first_half = shaped[:, :, :half_dim]
    second_half = shaped[:, :, half_dim:]
    turned = jnp.concatenate(
        [
            first_half * cosine - second_half * sine_part,
            second_half * cosine + first_half * sine_part,
        ],
        axis=2,
    )
    return turned.reshape(row_count, head_count * head_dim)


def token_layout(prompt_row, prefix_row, row_count):
    run_ends = jnp.cumsum(prompt_row, dtype=jnp.int32)
    starts = run_ends - prompt_row
    offsets = jnp.arange(row_count, dtype=jnp.int32)
    request = jnp.sum(
        (offsets[:, None] >= run_ends[None, :]).astype(jnp.int32), axis=1, dtype=jnp.int32
    )
    member = request[:, None] == jnp.arange(prompt_row.shape[0], dtype=jnp.int32)[None, :]
    start_of = jnp.sum(jnp.where(member, starts[None, :], 0), axis=1, dtype=jnp.int32)
    prefix_of = jnp.sum(jnp.where(member, prefix_row[None, :], 0), axis=1, dtype=jnp.int32)
    return (request, prefix_of + offsets - start_of)


def rescale(summed, factor):
    group_count, row_count, feature_width = summed.shape
    group_size = factor.shape[1]
    shaped = summed.reshape(group_count, row_count, group_size, feature_width // group_size)
    shaped = shaped * jnp.transpose(factor, (0, 2, 1))[:, :, :, None]
    return shaped.reshape(group_count, row_count, feature_width)


def divide_rows(summed, total_weight):
    group_count, row_count, feature_width = summed.shape
    group_size = total_weight.shape[1]
    shaped = summed.reshape(group_count, row_count, group_size, feature_width // group_size)
    shaped = shaped / jnp.transpose(total_weight, (0, 2, 1))[:, :, :, None]
    return shaped.reshape(group_count, row_count, feature_width)


def combine_parts(earlier_part, later_part):
    largest = jnp.maximum(earlier_part[0], later_part[0])
    factor_one = jnp.exp(earlier_part[0] - largest)
    factor_two = jnp.exp(later_part[0] - largest)
    total_weight = earlier_part[1] * factor_one + later_part[1] * factor_two
    summed = rescale(earlier_part[2], factor_one) + rescale(later_part[2], factor_two)
    return (largest, total_weight, summed)


def on_device(
    hidden_in,
    attn_gain,
    qkv_weight,
    out_weight,
    moe_gain,
    router_weight,
    expert_gate,
    expert_up,
    expert_down,
    cache_keys,
    cache_values,
    block_table,
    prefix_lengths,
    prompt_lengths,
    routed_experts,
):
    col_count = lax.axis_size("col")
    row_devices = lax.axis_size("row")
    col_index = lax.axis_index("col")
    row_index = lax.axis_index("row")
    tok_rows = hidden_in.shape[0]
    feature_width = hidden_in.shape[1]
    head_total = out_weight.shape[0]
    head_count = head_total // HEAD_DIM
    key_share = tok_rows // col_count
    request, position = token_layout(prompt_lengths[0], prefix_lengths[0], tok_rows)
    own_start = col_index * key_share
    key_position = lax.dynamic_slice_in_dim(position, own_start, key_share)
    key_request = lax.dynamic_slice_in_dim(request, own_start, key_share)
    residual = hidden_in.astype(jnp.float32)
    squares = lax.psum(jnp.sum(residual * residual, axis=1), "col")
    scale_one = lax.rsqrt(squares / D + norm_epsilon)
    normed = (residual * scale_one[:, None] * attn_gain[None, :]).astype(jnp.bfloat16)
    query_part = jnp.dot(normed, qkv_weight[:, :head_total], preferred_element_type=jnp.float32)
    query_sum = lax.psum(query_part, "col")
    queries = (rotate(query_sum, position, HEAD_DIM) * HEAD_DIM ** (-0.5)).astype(jnp.bfloat16)
    key_value = lax.psum_scatter(
        jnp.dot(normed, qkv_weight[:, head_total:], preferred_element_type=jnp.float32).astype(
            jnp.bfloat16
        ),
        "col",
        scatter_dimension=0,
        tiled=True,
    ).astype(jnp.float32)
    new_keys = rotate(key_value[:, :head_total], key_position, HEAD_DIM).astype(jnp.bfloat16)
    new_values = key_value[:, head_total:].astype(jnp.bfloat16)
    pool_size = cache_keys.shape[0]
    page_size = cache_keys.shape[1]
    req_count = block_table.shape[1]
    pages_each = block_table.shape[2] // col_count
    page_table = block_table[0].reshape(req_count, pages_each, col_count)
    own_pages = lax.dynamic_slice_in_dim(page_table, col_index, 1, 2).reshape(
        req_count * pages_each
    )
    pool_offset_begin = (row_index * col_count + col_index) * pool_size
    slot_ids = jnp.arange(pool_size, dtype=jnp.int32)
    entry_ids = jnp.arange(req_count * pages_each, dtype=jnp.int32)
    slot_match = (own_pages - pool_offset_begin)[None, :] == slot_ids[:, None]
    entry_request = entry_ids // pages_each
    entry_page = entry_ids % pages_each * col_count + col_index
    slot_request = jnp.sum(
        jnp.where(slot_match, entry_request[None, :], 0), axis=1, dtype=jnp.int32
    )
    slot_page = jnp.sum(jnp.where(slot_match, entry_page[None, :], 0), axis=1, dtype=jnp.int32)
    prefix_row = prefix_lengths[0]
    slot_prefix = jnp.sum(
        jnp.where(
            slot_request[:, None] == jnp.arange(req_count, dtype=jnp.int32)[None, :],
            prefix_row[None, :],
            0,
        ),
        axis=1,
        dtype=jnp.int32,
    )
    cache_position = (
        slot_page[:, None] * page_size + jnp.arange(page_size, dtype=jnp.int32)[None, :]
    )
    cache_live = (
        (cache_position < slot_prefix[:, None]).astype(jnp.int32).reshape(pool_size * page_size)
    )
    cache_request = jnp.broadcast_to(slot_request[:, None], (pool_size, page_size)).reshape(
        pool_size * page_size
    )
    cache_mask = (request[:, None] == cache_request[None, :]) & (cache_live[None, :] > 0)
    fresh_mask = (request[:, None] == key_request[None, :]) & (
        key_position[None, :] <= position[:, None]
    )
    group_size = math.gcd(head_count, 4)
    group_count = head_count // group_size
    query_heads = queries.reshape(tok_rows, head_count, HEAD_DIM)
    cached_key_heads = cache_keys.reshape(pool_size * page_size, head_count, HEAD_DIM)
    cached_value_heads = cache_values.reshape(pool_size * page_size, head_count, HEAD_DIM)
    fresh_key_heads = new_keys.reshape(key_share, head_count, HEAD_DIM)
    fresh_value_heads = new_values.reshape(key_share, head_count, HEAD_DIM)

    def head_group(group_index):
        first_head = group_index * group_size
        query_piece = lax.dynamic_slice_in_dim(query_heads, first_head, group_size, 1)
        key_piece = lax.dynamic_slice_in_dim(cached_key_heads, first_head, group_size, 1)
        value_piece = lax.dynamic_slice_in_dim(cached_value_heads, first_head, group_size, 1)
        fresh_key_piece = lax.dynamic_slice_in_dim(fresh_key_heads, first_head, group_size, 1)
        fresh_value_piece = lax.dynamic_slice_in_dim(fresh_value_heads, first_head, group_size, 1)
        score_matrix = jnp.einsum(
            "thd,khd->htk", query_piece, key_piece, preferred_element_type=jnp.float32
        )
        score_matrix = jnp.where(cache_mask[None], score_matrix, masked_score)
        fresh_scores = jnp.einsum(
            "thd,khd->htk", query_piece, fresh_key_piece, preferred_element_type=jnp.float32
        )
        fresh_scores = jnp.where(fresh_mask[None], fresh_scores, masked_score)
        largest = jnp.maximum(jnp.max(score_matrix, axis=2), jnp.max(fresh_scores, axis=2))
        cached_exp = jnp.where(cache_mask[None], jnp.exp(score_matrix - largest[:, :, None]), 0.0)
        fresh_exp = jnp.where(fresh_mask[None], jnp.exp(fresh_scores - largest[:, :, None]), 0.0)
        total_weight = jnp.sum(cached_exp, axis=2) + jnp.sum(fresh_exp, axis=2)
        summed = jnp.einsum(
            "htk,khd->thd",
            cached_exp.astype(jnp.bfloat16),
            value_piece,
            preferred_element_type=jnp.float32,
        )
        summed = summed + jnp.einsum(
            "htk,khd->thd",
            fresh_exp.astype(jnp.bfloat16),
            fresh_value_piece,
            preferred_element_type=jnp.float32,
        )
        return (largest, total_weight, summed.reshape(tok_rows, group_size * HEAD_DIM))

    largest, total_weight, summed = lax.map(head_group, jnp.arange(group_count, dtype=jnp.int32))
    largest, total_weight, summed = merged((largest, total_weight, summed), "col", combine_parts)
    attended = divide_rows(summed, total_weight).astype(jnp.bfloat16)
    projected = jnp.einsum(
        "gtx,gxo->to",
        attended,
        out_weight.reshape(group_count, group_size * HEAD_DIM, feature_width),
        preferred_element_type=jnp.float32,
    )
    attn_out = projected.astype(jnp.bfloat16)
    middle = (residual + residual_scale * attn_out.astype(jnp.float32)).astype(jnp.bfloat16)
    middle_wide = middle.astype(jnp.float32)
    squares_two = lax.psum(jnp.sum(middle_wide * middle_wide, axis=1), "col")
    scale_two = lax.rsqrt(squares_two / D + norm_epsilon)
    moe_normed_f = middle_wide * scale_two[:, None] * moe_gain[None, :]
    logits = lax.psum(jnp.dot(moe_normed_f, router_weight, precision=lax.Precision.HIGHEST), "col")
    moe_normed = moe_normed_f.astype(jnp.bfloat16)
    expert_local = expert_gate.shape[0]
    expert_total = expert_local * row_devices
    capacity = 2 * TOP * tok_rows // expert_total
    onehot_three = (
        routed_experts[:, :, None] == jnp.arange(expert_total, dtype=jnp.int32)[None, None, :]
    )
    selected_logits = jnp.sum(jnp.where(onehot_three, logits[:, None, :], 0.0), axis=2)
    first_gate = jax.nn.sigmoid(selected_logits[:, 0] - selected_logits[:, 1])
    gate_pair = jnp.stack([first_gate, 1.0 - first_gate], axis=1)
    onehot = onehot_three.astype(jnp.int32).reshape(tok_rows * TOP, expert_total)
    earlier = jnp.cumsum(onehot, axis=0, dtype=jnp.int32) - onehot
    slot_index = jnp.sum(earlier * onehot, axis=1, dtype=jnp.int32)
    target = routed_experts.reshape(tok_rows * TOP) * capacity + slot_index
    token_local = jnp.arange(tok_rows * TOP, dtype=jnp.int32) // TOP
    source = jnp.zeros((expert_total * capacity,), jnp.int32).at[target].set(token_local)
    filled = jnp.zeros((expert_total * capacity,), jnp.int32).at[target].set(1)
    outgoing = jnp.where(
        filled[:, None] > 0, moe_normed[source], jnp.zeros((), jnp.bfloat16)
    ).reshape(expert_total, capacity, feature_width)
    arrived = lax.all_to_all(outgoing, "row", split_axis=0, concat_axis=0, tiled=True)
    expert_rows = (
        arrived.reshape(row_devices, expert_local, capacity, feature_width)
        .transpose(1, 0, 2, 3)
        .reshape(expert_local, row_devices * capacity, feature_width)
    )
    feature_piece = lax.all_gather(expert_rows, "col", axis=2, tiled=True)
    gate_next = jnp.einsum(
        "erd,edf->erf", feature_piece, expert_gate, preferred_element_type=jnp.float32
    )
    up_next = jnp.einsum(
        "erd,edf->erf", feature_piece, expert_up, preferred_element_type=jnp.float32
    )
    hidden = (jax.nn.silu(gate_next) * up_next).astype(jnp.bfloat16)
    received_rows = hidden.shape[1]
    value_partial_sum = jnp.einsum(
        "efo,erf->oer", expert_down, hidden, preferred_element_type=jnp.float32
    )
    expert_out = lax.psum_scatter(
        value_partial_sum.reshape(
            lax.axis_size("col") * feature_width, expert_local * received_rows
        ).astype(jnp.bfloat16),
        "col",
        scatter_dimension=0,
        tiled=True,
    )
    returned = lax.all_to_all(
        expert_out.reshape(feature_width, expert_local, received_rows),
        "row",
        split_axis=2,
        concat_axis=1,
        tiled=True,
    )
    flat_back = returned.reshape(feature_width, expert_total * capacity)
    picked = (
        jnp.take(flat_back, target, axis=1)
        .astype(jnp.float32)
        .reshape(feature_width, tok_rows, TOP)
    )
    moe_columns = jnp.sum(picked * gate_pair[None, :, :], axis=2).astype(jnp.bfloat16)
    moe_out = moe_columns.T
    layer_out = (middle_wide + residual_scale * moe_out.astype(jnp.float32)).astype(jnp.bfloat16)
    return (attn_out, moe_out, layer_out)


def solution(mesh):
    in_specs = (
        P("row", "col"),
        P("col"),
        P("col", None),
        P(None, "col"),
        P("col"),
        P("col", None),
        P("row", None, "col"),
        P("row", None, "col"),
        P("row", "col", None),
        P(("row", "col"), None, None),
        P(("row", "col"), None, None),
        P("row", None, None),
        P("row", None),
        P("row", None),
        P("row", None),
    )
    out_specs = (P("row", "col"), P("row", "col"), P("row", "col"))
    return jax.shard_map(
        on_device, mesh=mesh, in_specs=in_specs, out_specs=out_specs, check_vma=False
    )
```

profile of v0, /device:TPU:2, one launch (start us, length us, event | category | flops | bytes accessed | tf_op | source)
XLA Modules:
  0.0 942.3 jit_solution(6926186442801343392)
XLA Ops:
  8.0 62.3 %psum.28 = f32[128]{0:T(128)S(1)} all-reduce(f32[128]{0:T(128)S(1)} %fusion.64), channel_id=1, replica_groups=mesh['row'=8,'col'=32] {'col'}, use_global_device_ids=true, to_apply=%region_1.2 | all-reduce | flops 128 | bytes 1024 | tf_op jit(solution)/shard_map/psum | solution.py:114
  70.3 2.7 convolution_convert_fusion
  77.7 5.0 reshape.454
  82.7 6.9 copy.162
  89.5 5.0 reshape.455
  94.5 6.7 copy.163
  102.5 88.4 %all-reduce.6.cloned.1.call-done = bf16[128,4608]{1,0:T(8,128)(2,1)} async-done(((bf16[128,4608]{1,0:T(8,128)(2,1)}), bf16[128,4608]{1,0:T(8,128)(2,1)}) %all-reduce.6.cloned.1.call-update) | async-done | bytes 1179664
  192.2 117.1 %all-reduce.4.cloned.1.call-done = f32[128,36,64]{0,2,1:T(8,128)} async-done(((f32[128,36,64]{0,2,1:T(8,128)}), f32[128,36,64]{0,2,1:T(8,128)}) %all-reduce.4.cloned.1.call-update) | async-done | bytes 1179664 | tf_op jit(solution)/shard_map/psum | solution.py:118
  310.9 51.9 %while.31 = (s32[]{:T(128)}, f32[9,4,128]{2,1,0:T(4,128)S(1)}, f32[9,4,128]{2,1,0:T(4,128)S(1)}, f32[9,128,256]{2,1,0:T(8,128)}, s32[9]{0:T(128)S(1)}, /*index=5...) while((s32[]{:T(128)}, f32[9,4,128]{2,1,0:T(4,128)S(1)}, ...), condition=%wide.region_16.17_spmd.clone.clone, body=%wide.region_11.16_spmd.clone.clone.sunk | while | flops 69911040 | bytes 5058339 | solution.py:212
  368.0 24.4 %all-gather = f32[288,4,128]{2,1,0:T(4,128)S(1)} all-gather(f32[9,4,128]{2,1,0:T(4,128)S(1)} %get-tuple-element.105), channel_id=2, replica_groups=mesh['row'=8,'col'=32] {'col'}, dimensions={0}, use_global_device_ids=true | all-gather | bytes 608256 | tf_op jit(solution)/shard_map/all_gather | solution.py:17
  392.5 25.6 %all-gather.1 = f32[288,4,128]{2,1,0:T(4,128)S(1)} all-gather(f32[9,4,128]{2,1,0:T(4,128)S(1)} %get-tuple-element.106), channel_id=3, replica_groups=mesh['row'=8,'col'=32] {'col'}, dimensions={0}, use_global_device_ids=true | all-gather | bytes 608256 | tf_op jit(solution)/shard_map/all_gather | solution.py:17
  418.2 76.0 %all-gather.8.cloned.1.call-done = f32[288,128,256]{2,1,0:T(8,128)} async-done(((f32[9,128,256]{2,1,0:T(8,128)}), f32[288,128,256]{2,1,0:T(8,128)}) %all-gather.8.cloned.1.call-update) | async-done | bytes 37748752 | tf_op jit(solution)/shard_map/all_gather | solution.py:17
  496.8 26.9 %slice.93 = f32[279,128,256]{2,1,0:T(8,128)} slice(f32[288,128,256]{2,1,0:T(8,128)} %all-gather.8.cloned.1.call-done), slice={[9:288], [0:128], [0:256]} | slice | bytes 73138176 | tf_op jit(solution)/shard_map/slice | solution.py:19
  523.7 168.2 %while.30 = (s32[]{:T(128)}, f32[9,4,128]{2,1,0:T(4,128)S(1)}, f32[9,4,128]{2,1,0:T(4,128)S(1)}, f32[9,128,256]{1,2,0:T(8,128)}, f32[31,9,4,128]{3,2,1,0:T(4,128...) while((s32[]{:T(128)}, f32[9,4,128]{2,1,0:T(4,128)S(1)}, ...), condition=%wide.region_18.19_spmd, body=%wide.region_17.18_spmd.sunk | while | flops 916994 | bytes 17676496 | solution.py:20
  526.5 2.6 fusion.111
  531.9 2.6 fusion.111
  537.4 2.6 fusion.111
  542.8 2.6 fusion.111
  548.2 2.6 fusion.111
  553.6 2.6 fusion.111
  559.1 2.6 fusion.111
  564.5 2.6 fusion.111
  569.9 2.6 fusion.111
  575.3 2.6 fusion.111
  580.8 2.6 fusion.111
  586.2 2.6 fusion.111
  591.6 2.6 fusion.111
  597.0 2.6 fusion.111
  602.5 2.6 fusion.111
  607.9 2.6 fusion.111
  613.3 2.6 fusion.111
  624.2 2.6 fusion.111
  635.0 2.6 fusion.111
  645.9 2.6 fusion.111
  651.3 2.6 fusion.111
  656.7 2.6 fusion.111
  662.2 2.6 fusion.111
  673.0 2.6 fusion.111
  683.9 2.6 fusion.111
  694.2 60.6 %psum.30 = f32[128]{0:T(128)S(1)} all-reduce(f32[128]{0:T(128)S(1)} %get-tuple-element.401), channel_id=1, replica_groups=mesh['row'=8,'col'=32] {'col'}, use_global_device_ids=true, to_apply=%region_24.25 | all-reduce | flops 128 | bytes 1024 | tf_op jit(solution)/shard_map/psum | solution.py:224
  756.5 15.9 %all_to_all.14 = bf16[8,64,72]{2,1,0:T(8,128)(2,1)S(1)} all-to-all(bf16[8,64,72]{2,1,0:T(8,128)(2,1)S(1)} %broadcast_select_fusion), channel_id=1, replica_groups=mesh['row'=8,'col'=32] {'row'}, dimensions={0} | all-to-all | bytes 147456 | tf_op jit(solution)/shard_map/all_to_all | solution.py:248
  773.2 44.9 %all-gather.6.cloned.1.call-done = bf16[1,512,2304]{1,2,0:T(8,128)(2,1)} async-done(((bf16[1,512,72]{1,2,0:T(8,128)(2,1)}), bf16[1,512,2304]{1,2,0:T(8,128)(2,1)}) %all-gather.6.cloned.1.call-update) | async-done | bytes 2359312 | tf_op jit(solution)/shard_map/all_gather | solution.py:254
  818.1 3.0 fusion.36
  821.2 3.4 fusion.33
  827.9 60.4 %psum.31 = f32[128,8]{0,1:T(8,128)S(1)} all-reduce(f32[128,8]{0,1:T(8,128)S(1)} %fusion.70), channel_id=1, replica_groups=mesh['row'=8,'col'=32] {'col'}, use_global_device_ids=true, to_apply=%region_27.28 | all-reduce | flops 1024 | bytes 8192 | tf_op jit(solution)/shard_map/psum | solution.py:227
  888.4 25.3 %reduce-scatter.4.cloned.1.call-done = bf16[72,512]{1,0:T(8,128)(2,1)} async-done(((bf16[2304,512]{1,0:T(8,128)(2,1)}), bf16[72,512]{1,0:T(8,128)(2,1)}) %reduce-scatter.4.cloned.1.call-update) | async-done | bytes 73744
  917.8 7.0 all-to-all-start.1
  925.0 8.3 all-to-all-done.1
  (671 shorter events, 177.2 us)
Async XLA Ops:
  7.2 814.0 %copy-start = (bf16[1,180,2304]{2,1,0:T(8,128)(2,1)S(1)}, bf16[1,180,2304]{2,1,0:T(8,128)(2,1)}, u32[]{:S(2)}) copy-start(bf16[1,180,2304]{2,1,0:T(8,128)(2,1)} %param.27) | copy-start | bytes 2488324
  7.2 183.7 %all-reduce.6.cloned.1.call-start = ((), (), s32[]{:S(2)}) async-start(), calls=%async_computation.7 | async-start | bytes 2359296
  70.3 2.9 copy-start.8
  70.3 2.9 copy-start.12
  73.1 2.9 copy-start.17
  73.1 3.2 copy-start.14
  73.1 3.4 copy-start.11
  73.1 4.6 copy-start.1
  73.1 236.2 %all-reduce.4.cloned.1.call-start = ((), (), s32[]{:S(2)}) async-start(), calls=%async_computation.3 | async-start | bytes 2359296 | tf_op jit(solution)/shard_map/psum | solution.py:118
  75.8 418.3 %all-gather.8.cloned.1.call-start = ((), (), s32[]{:S(2)}) async-start(), calls=%async_computation.5 | async-start | bytes 38928384 | tf_op jit(solution)/shard_map/all_gather | solution.py:17
  82.7 6.9 copy-start.2
  94.5 6.7 copy-start.18
  362.8 455.3 %all-gather.6.cloned.1.call-start = ((), (), s32[]{:S(2)}) async-start(), calls=%async_computation.4 | async-start | bytes 2433024 | tf_op jit(solution)/shard_map/all_gather | solution.py:254
  526.5 2.6 copy-start.4
  531.9 2.6 copy-start.4
  537.3 2.6 copy-start.4
  542.8 2.6 copy-start.4
  548.2 2.6 copy-start.4
  553.6 2.6 copy-start.4
  559.0 2.6 copy-start.4
  564.5 2.6 copy-start.4
  569.9 2.6 copy-start.4
  575.3 2.6 copy-start.4
  580.7 2.6 copy-start.4
  586.2 2.6 copy-start.4
  591.6 2.6 copy-start.4
  597.0 2.6 copy-start.4
  602.4 2.6 copy-start.4
  607.9 2.6 copy-start.4
  613.3 2.6 copy-start.4
  618.7 2.6 copy-start.4
  624.1 2.6 copy-start.4
  629.6 2.6 copy-start.4
  635.0 2.6 copy-start.4
  640.4 2.6 copy-start.4
  645.9 2.6 copy-start.4
  651.3 2.6 copy-start.4
  656.7 2.6 copy-start.4
  662.1 2.6 copy-start.4
  667.6 2.6 copy-start.4
  673.0 2.6 copy-start.4
  678.4 2.6 copy-start.4
  683.8 2.6 copy-start.4
  689.3 2.6 copy-start.4
  691.9 62.9 %copy-start.13 = (f32[72]{0:T(128)S(1)}, f32[72]{0:T(128)}, u32[]{:S(2)}) copy-start(f32[72]{0:T(128)} %param.23) | copy-start | bytes 868
  694.2 123.9 %copy-start.15 = (bf16[1,2304,180]{1,2,0:T(8,128)(2,1)S(1)}, bf16[1,2304,180]{1,2,0:T(8,128)(2,1)}, u32[]{:S(2)}) copy-start(bf16[1,2304,180]{1,2,0:T(8,128)(2,1)} %param.25) | copy-start | bytes 2488324
  773.1 140.5 %reduce-scatter.4.cloned.1.call-start = ((), (), s32[]{:S(2)}) async-start(), calls=%async_computation.6 | async-start | bytes 2433024
  917.8 15.5 %all-to-all-start.1 = ((bf16[8,2,2304]{2,1,0:T(2,128)(2,1)}), bf16[8,2,2304]{2,1,0:T(2,128)(2,1)S(1)}, u32[]{:S(2)}, u32[]{:S(2)}) async-start(bf16[8,2,2304]{2,1,0:T(2,128)(2,1)} %reshape.465), calls=%async_computation.1 | async-start | bytes 147456 | tf_op jit(solution)/shard_map/all_to_all | solution.py:274
  (98 other events, 142.4 us)
Sparse Core Ops, SparseCore 0:
  73.2 117.6 all-reduce.5
  194.2 115.0 all-reduce.3
  362.9 131.1 all-gather.7
  773.3 44.8 all-gather.5
  827.2 86.4 reduce-scatter.3
where the time goes:
time: 946 us; the launch traced here: 942 us
  waiting for transfers between devices  360 us (38%)
  blocking collectives  249 us (26%)
  local copies, waits for them, and re-layouts  164 us (17%)
  other arithmetic  97.8 us (10%)
  matrix products  40.8 us (4%)
  between operations  14.9 us (2%)
    psum x1, waiting for transfers between devices, on_device(): query_sum = lax.psum(query_part, 'col')  117 us
    unnamed x7, waiting for transfers between devices  114 us
    add x31, other arithmetic, combine_parts(): rescale(earlier_part[2], factor_one) + rescale(later_part[2], factor_two)  81.3 us
    all_gather x1, waiting for transfers between devices, merged(): pieces = jax.tree.map(lambda part: lax.all_gather(part, axis), value)  76 us
    psum x1, blocking collectives, on_device(): squares = lax.psum(jnp.sum(residual * residual, axis=1), 'col')  62.3 us
    psum x1, blocking collectives, on_device(): squares_two = lax.psum(jnp.sum(middle_wide * middle_wide, axis=1), 'col')  60.6 us
    psum x1, blocking collectives, on_device(): lax.psum(jnp.dot(moe_normed_f, router_weight, precision=lax.Precision.HIG...  60.4 us
    dynamic_slice x62, local copies, waits for them, and re-layouts, merged(): lax.scan(lambda running, slab: (join(running, slab), None), head, tail)  53.9 us
  transfers between devices with their start and end apart: 6, of which 6 were waited for; matrix products, arithmetic and copies ran while one was open for 4% of the time, Pallas kernels for 0%

commit v1 on v0

--- a/solution.py
+++ b/solution.py
@@ -251,7 +251,9 @@
         .transpose(1, 0, 2, 3)
         .reshape(expert_local, row_devices * capacity, feature_width)
     )
-    feature_piece = lax.all_gather(expert_rows, "col", axis=2, tiled=True)
+    feature_piece = jnp.concatenate(
+        lax.all_to_all(jnp.stack([expert_rows] * lax.axis_size("col")), "col", 0, 0), axis=2
+    )
     gate_next = jnp.einsum(
         "erd,edf->erf", feature_piece, expert_gate, preferred_element_type=jnp.float32
     )

time: 946 us -> 934 us (0.987)
  waiting for transfers between devices: 360 us -> 309 us
  blocking collectives: 249 us -> 288 us
    all_gather x1 -> x0, waiting for transfers between devices: 44.9 us -> none  [on_device(): feature_piece = lax.all_gather(expert_rows, 'col', axis=2, tiled=True)]
    all_to_all x0 -> x1, blocking collectives: none -> 38.5 us  [on_device(): lax.all_to_all(jnp.stack([expert_rows] * lax.axis_size('col')), 'col', 0, 0)]
    unnamed x7 -> x6, waiting for transfers between devices: 114 us -> 108 us
  transfers between devices with their start and end apart: 6 -> 5, of which waited for: 6 -> 5; matrix products, arithmetic and copies ran while one was open for 4% -> 4% of each run, Pallas kernels for 0% -> 0%
where the time goes in v1:
time: 934 us; the launch traced here: 930 us
  waiting for transfers between devices  309 us (33%)
  blocking collectives  288 us (31%)
  local copies, waits for them, and re-layouts  165 us (18%)
  other arithmetic  97.8 us (10%)
  matrix products  39.9 us (4%)
  between operations  14.9 us (2%)
    psum x1, waiting for transfers between devices, on_device(): query_sum = lax.psum(query_part, 'col')  117 us
    unnamed x6, waiting for transfers between devices  108 us
    add x31, other arithmetic, combine_parts(): rescale(earlier_part[2], factor_one) + rescale(later_part[2], factor_two)  81.3 us
    all_gather x1, waiting for transfers between devices, merged(): pieces = jax.tree.map(lambda part: lax.all_gather(part, axis), value)  76 us
    psum x1, blocking collectives, on_device(): squares = lax.psum(jnp.sum(residual * residual, axis=1), 'col')  62.3 us
    psum x1, blocking collectives, on_device(): lax.psum(jnp.dot(moe_normed_f, router_weight, precision=lax.Precision.HIG...  60.5 us
    psum x1, blocking collectives, on_device(): squares_two = lax.psum(jnp.sum(middle_wide * middle_wide, axis=1), 'col')  60.4 us
    dynamic_slice x62, local copies, waits for them, and re-layouts, merged(): lax.scan(lambda running, slab: (join(running, slab), None), head, tail)  53.9 us
  transfers between devices with their start and end apart: 5, of which 5 were waited for; matrix products, arithmetic and copies ran while one was open for 4% of the time, Pallas kernels for 0%

profile of v1, /device:TPU:2, one launch (start us, length us, event | category | flops | bytes accessed | tf_op | source)
XLA Modules:
  0.0 930.1 jit_solution(11281973681035238674)
XLA Ops:
  8.0 62.3 %psum.28 = f32[128]{0:T(128)S(1)} all-reduce(f32[128]{0:T(128)S(1)} %fusion.54), channel_id=1, replica_groups=mesh['row'=8,'col'=32] {'col'}, use_global_device_ids=true, to_apply=%region_1.2 | all-reduce | flops 128 | bytes 1024 | tf_op jit(solution)/shard_map/psum | solution.py:114
  70.3 2.7 convolution_convert_fusion
  77.7 5.0 reshape.465
  82.7 6.9 copy.144
  89.5 5.0 reshape.466
  94.5 6.7 copy.145
  102.5 88.4 %all-reduce.6.cloned.1.call-done = bf16[128,4608]{1,0:T(8,128)(2,1)} async-done(((bf16[128,4608]{1,0:T(8,128)(2,1)}), bf16[128,4608]{1,0:T(8,128)(2,1)}) %all-reduce.6.cloned.1.call-update) | async-done | bytes 1179664
  192.2 117.1 %all-reduce.4.cloned.1.call-done = f32[128,36,64]{0,2,1:T(8,128)} async-done(((f32[128,36,64]{0,2,1:T(8,128)}), f32[128,36,64]{0,2,1:T(8,128)}) %all-reduce.4.cloned.1.call-update) | async-done | bytes 1179664 | tf_op jit(solution)/shard_map/psum | solution.py:118
  310.9 51.9 %while.31 = (s32[]{:T(128)}, f32[9,4,128]{2,1,0:T(4,128)S(1)}, f32[9,4,128]{2,1,0:T(4,128)S(1)}, f32[9,128,256]{2,1,0:T(8,128)}, s32[9]{0:T(128)S(1)}, /*index=5...) while((s32[]{:T(128)}, f32[9,4,128]{2,1,0:T(4,128)S(1)}, ...), condition=%wide.region_16.17_spmd.clone.clone, body=%wide.region_11.16_spmd.clone.clone.sunk | while | flops 69911040 | bytes 5058339 | solution.py:212
  368.0 24.4 %all-gather = f32[288,4,128]{2,1,0:T(4,128)S(1)} all-gather(f32[9,4,128]{2,1,0:T(4,128)S(1)} %get-tuple-element.105), channel_id=2, replica_groups=mesh['row'=8,'col'=32] {'col'}, dimensions={0}, use_global_device_ids=true | all-gather | bytes 608256 | tf_op jit(solution)/shard_map/all_gather | solution.py:17
  392.5 25.6 %all-gather.1 = f32[288,4,128]{2,1,0:T(4,128)S(1)} all-gather(f32[9,4,128]{2,1,0:T(4,128)S(1)} %get-tuple-element.106), channel_id=3, replica_groups=mesh['row'=8,'col'=32] {'col'}, dimensions={0}, use_global_device_ids=true | all-gather | bytes 608256 | tf_op jit(solution)/shard_map/all_gather | solution.py:17
  418.2 76.0 %all-gather.5.cloned.1.call-done = f32[288,128,256]{2,1,0:T(8,128)} async-done(((f32[9,128,256]{2,1,0:T(8,128)}), f32[288,128,256]{2,1,0:T(8,128)}) %all-gather.5.cloned.1.call-update) | async-done | bytes 37748752 | tf_op jit(solution)/shard_map/all_gather | solution.py:17
  496.8 26.9 %slice.93 = f32[279,128,256]{2,1,0:T(8,128)} slice(f32[288,128,256]{2,1,0:T(8,128)} %all-gather.5.cloned.1.call-done), slice={[9:288], [0:128], [0:256]} | slice | bytes 73138176 | tf_op jit(solution)/shard_map/slice | solution.py:19
  523.7 168.2 %while.30 = (s32[]{:T(128)}, f32[9,4,128]{2,1,0:T(4,128)S(1)}, f32[9,4,128]{2,1,0:T(4,128)S(1)}, f32[9,128,256]{1,2,0:T(8,128)}, f32[31,9,4,128]{3,2,1,0:T(4,128...) while((s32[]{:T(128)}, f32[9,4,128]{2,1,0:T(4,128)S(1)}, ...), condition=%wide.region_18.19_spmd, body=%wide.region_17.18_spmd.sunk | while | flops 916994 | bytes 17676496 | solution.py:20
  526.5 2.6 fusion.103
  531.9 2.6 fusion.103
  537.4 2.6 fusion.103
  542.8 2.6 fusion.103
  548.2 2.6 fusion.103
  553.6 2.6 fusion.103
  559.1 2.6 fusion.103
  564.5 2.6 fusion.103
  569.9 2.6 fusion.103
  575.3 2.6 fusion.103
  580.8 2.6 fusion.103
  586.2 2.6 fusion.103
  591.6 2.6 fusion.103
  597.0 2.6 fusion.103
  602.5 2.6 fusion.103
  607.9 2.6 fusion.103
  613.3 2.6 fusion.103
  624.2 2.6 fusion.103
  635.0 2.6 fusion.103
  645.9 2.6 fusion.103
  651.3 2.6 fusion.103
  656.7 2.6 fusion.103
  662.2 2.6 fusion.103
  673.0 2.6 fusion.103
  683.9 2.6 fusion.103
  694.2 60.4 %psum.30 = f32[128]{0:T(128)S(1)} all-reduce(f32[128]{0:T(128)S(1)} %get-tuple-element.378), channel_id=1, replica_groups=mesh['row'=8,'col'=32] {'col'}, use_global_device_ids=true, to_apply=%region_24.25 | all-reduce | flops 128 | bytes 1024 | tf_op jit(solution)/shard_map/psum | solution.py:224
  756.4 15.9 %all_to_all.19 = bf16[8,64,72]{2,1,0:T(8,128)(2,1)S(1)} all-to-all(bf16[8,64,72]{2,1,0:T(8,128)(2,1)S(1)} %broadcast_select_fusion), channel_id=1, replica_groups=mesh['row'=8,'col'=32] {'row'}, dimensions={0} | all-to-all | bytes 147456 | tf_op jit(solution)/shard_map/all_to_all | solution.py:248
  772.5 38.5 %all_to_all.20 = bf16[32,1,512,72]{2,3,1,0:T(8,128)(2,1)S(1)} all-to-all(bf16[32,1,512,72]{2,3,1,0:T(8,128)(2,1)S(1)} %stack.8), channel_id=1, replica_groups=mesh['row'=8,'col'=32] {'col'}, dimensions={0} | all-to-all | bytes 4718592 | tf_op jit(solution)/shard_map/all_to_all | solution.py:255
  812.4 4.1 fusion.33
  816.5 4.3 copy.147
  821.7 60.5 %psum.31 = f32[128,8]{0,1:T(8,128)S(1)} all-reduce(f32[128,8]{0,1:T(8,128)S(1)} %fusion.60), channel_id=1, replica_groups=mesh['row'=8,'col'=32] {'col'}, use_global_device_ids=true, to_apply=%region_27.28 | all-reduce | flops 1024 | bytes 8192 | tf_op jit(solution)/shard_map/psum | solution.py:227
  882.2 19.3 %reduce-scatter.4.cloned.1.call-done = bf16[72,512]{1,0:T(8,128)(2,1)} async-done(((bf16[2304,512]{1,0:T(8,128)(2,1)}), bf16[72,512]{1,0:T(8,128)(2,1)}) %reduce-scatter.4.cloned.1.call-update) | async-done | bytes 73744
  905.6 7.0 all-to-all-start.2
  912.7 8.3 all-to-all-done.2
  (670 shorter events, 175.6 us)
Async XLA Ops:
  7.2 805.3 %copy-start = (bf16[1,180,2304]{2,1,0:T(8,128)(2,1)S(1)}, bf16[1,180,2304]{2,1,0:T(8,128)(2,1)}, u32[]{:S(2)}) copy-start(bf16[1,180,2304]{2,1,0:T(8,128)(2,1)} %param.27) | copy-start | bytes 2488324
  7.2 183.7 %all-reduce.6.cloned.1.call-start = ((), (), s32[]{:S(2)}) async-start(), calls=%async_computation.7 | async-start | bytes 2359296
  70.3 2.9 copy-start.8
  70.3 2.9 copy-start.12
  73.1 2.9 copy-start.17
  73.1 3.2 copy-start.14
  73.1 3.4 copy-start.11
  73.1 4.6 copy-start.1
  73.1 236.2 %all-reduce.4.cloned.1.call-start = ((), (), s32[]{:S(2)}) async-start(), calls=%async_computation.4 | async-start | bytes 2359296 | tf_op jit(solution)/shard_map/psum | solution.py:118
  75.8 418.3 %all-gather.5.cloned.1.call-start = ((), (), s32[]{:S(2)}) async-start(), calls=%async_computation.5 | async-start | bytes 38928384 | tf_op jit(solution)/shard_map/all_gather | solution.py:17
  82.7 6.9 copy-start.2
  94.5 6.7 copy-start.18
  362.8 538.7 %reduce-scatter.4.cloned.1.call-start = ((), (), s32[]{:S(2)}) async-start(), calls=%async_computation.6 | async-start | bytes 2433024
  526.5 2.6 copy-start.4
  531.9 2.6 copy-start.4
  531.9 2.6 copy-start.6
  537.3 2.6 copy-start.4
  542.8 2.6 copy-start.4
  548.2 2.6 copy-start.4
  553.6 2.6 copy-start.4
  559.0 2.6 copy-start.4
  564.5 2.6 copy-start.4
  569.9 2.6 copy-start.4
  575.3 2.6 copy-start.4
  580.7 2.6 copy-start.4
  586.2 2.6 copy-start.4
  591.6 2.6 copy-start.4
  597.0 2.6 copy-start.4
  602.4 2.6 copy-start.4
  607.9 2.6 copy-start.4
  613.3 2.6 copy-start.4
  618.7 2.6 copy-start.4
  624.1 2.6 copy-start.4
  629.6 2.6 copy-start.4
  635.0 2.6 copy-start.4
  640.4 2.6 copy-start.4
  645.9 2.6 copy-start.4
  651.3 2.6 copy-start.4
  656.7 2.6 copy-start.4
  662.1 2.6 copy-start.4
  667.6 2.6 copy-start.4
  673.0 2.6 copy-start.4
  678.4 2.6 copy-start.4
  683.8 2.6 copy-start.4
  689.3 2.6 copy-start.4
  691.9 62.8 %copy-start.13 = (f32[72]{0:T(128)S(1)}, f32[72]{0:T(128)}, u32[]{:S(2)}) copy-start(f32[72]{0:T(128)} %param.23) | copy-start | bytes 868
  772.5 38.5 %copy-start.15 = (bf16[1,2304,180]{1,2,0:T(8,128)(2,1)S(1)}, bf16[1,2304,180]{1,2,0:T(8,128)(2,1)}, u32[]{:S(2)}) copy-start(bf16[1,2304,180]{1,2,0:T(8,128)(2,1)} %param.25) | copy-start | bytes 2488324
  905.6 15.4 %all-to-all-start.2 = ((bf16[8,2,2304]{2,1,0:T(2,128)(2,1)}), bf16[8,2,2304]{2,1,0:T(2,128)(2,1)S(1)}, u32[]{:S(2)}, u32[]{:S(2)}) async-start(bf16[8,2,2304]{2,1,0:T(2,128)(2,1)} %reshape.476), calls=%async_computation.2 | async-start | bytes 147456 | tf_op jit(solution)/shard_map/all_to_all | solution.py:276
  (97 other events, 139.8 us)
Sparse Core Ops, SparseCore 0:
  73.2 117.6 all-reduce.5
  194.2 115.0 all-reduce.3
  362.9 131.1 all-gather.4
  821.0 80.5 reduce-scatter.3
